TPU v7x, 512 devices: a whole 4x4x16 slice. The times are simulated.
512 devices in a mesh: blk: 64 (over y_lo, z, core), exp: 8 (over y_hi, x).
Axes of the slice: x: 4, y: 4 (y_hi: 2, y_lo: 2; y = y_hi * 2 + y_lo), z: 16, core: 2. Of those that a mesh axis runs over, the one named last changes fastest.
Arguments:
- hidden_in: bfloat16 [32, 4, 2048], P('exp'), may hold values from -3 to 3
- q_lat: bfloat16 [32, 4, 16, 512], P('exp'), may hold values from -28 to 28
- q_rope: bfloat16 [32, 4, 16, 64], P('exp'), may hold values from -4 to 4
- new_lat: bfloat16 [32, 4, 512], P('exp'), may hold values from -4 to 4
- new_rope: bfloat16 [32, 4, 64], P('exp'), may hold values from -4 to 4
- cache_lat: bfloat16 [32, 16384, 512], P('exp', 'blk'), may hold values from -4 to 4
- cache_rope: bfloat16 [32, 16384, 64], P('exp', 'blk'), may hold values from -4 to 4
- lengths: int32 [32], P('exp'), may hold values from 2 to 16384, as said below
- w_uv: bfloat16 [512, 2048], P(None, 'blk'), may hold values from -3 to 3
- w_out: bfloat16 [2048, 2048], P('blk'), may hold values from -0.125 to 0.125
- norm_gain: float32 [2048], replicated, may hold values from 0.1 to 1.9
- w_router: bfloat16 [2048, 64], replicated, may hold values from -0.125 to 0.125
- routes: int32 [32, 4, 6], P('exp'), may hold values from 0 to 63, all different within a row; in each aligned block of 16 rows (0 to 15, 16 to 31, ..., all dimensions but the last counted through in order) at most 3 rows name the same one
- w_gate: bfloat16 [64, 2048, 1408], P('blk', None, 'exp'), may hold values from -0.125 to 0.125
- w_up: bfloat16 [64, 2048, 1408], P('blk', None, 'exp'), may hold values from -0.125 to 0.125
- w_down: bfloat16 [64, 1408, 2048], P('blk', 'exp'), may hold values from -0.15625 to 0.15625
Outputs:
- hidden_out: bfloat16 [32, 4, 2048], P('exp')
Inputs may be any that keep to these rules, and one draw needn't show every extreme that they name: `lengths`: in each aligned group of 4 requests exactly 1 have length 16384; the others have 2 to 512. `routes`: each row names 6 different experts; in the 16 rows of one index of exp no expert is named more than 3 times.
All inputs are finite; a program needn't handle non-finite values.
Results may differ from a plain program's by a relative error of at most 0.0062.
Values may be sent and summed in bfloat16 or wider, within the bound.
No kernel may reach another device: no remote copies, remote signals or barrier semaphores. Data moves between devices by JAX's collectives and lax.ppermute only.
A program may use at most 128 MiB of HBM per device.

v0:
```python
import jax
import jax.numpy as jnp
from jax import lax
from jax.sharding import PartitionSpec as P

V = 128
QK = 192
CAP = 3
NEG_FILL = -1e30
ROUTE_SCALE = 2.446
NORM_EPS = 1e-06


def merged_2(x, axis, combine):
    everything = jax.tree.map(lambda part: lax.all_gather(part, axis), x)
    leading = jax.tree.map(lambda part: part[0], everything)

    def step(k, so_far):
        return combine(so_far, jax.tree.map(lambda part: part[k], everything))

    return lax.fori_loop(1, lax.axis_size(axis), step, leading)


def block_partial(query, query_rope, keys_lat, keys_rope, valid):
    scale = QK ** (-0.5)
    scores = (
        jnp.einsum("rmc,rkc->rmk", query, keys_lat, preferred_element_type=jnp.float32)
        + jnp.einsum("rmc,rkc->rmk", query_rope, keys_rope, preferred_element_type=jnp.float32)
    ) * scale
    masked = jnp.where(valid, scores, NEG_FILL)
    peak_val = jnp.max(masked, axis=2)
    weights = jnp.where(valid, jnp.exp(masked - peak_val[:, :, None]), 0.0)
    weight_sum = jnp.sum(weights, axis=2)
    summed = jnp.einsum(
        "rmk,rkc->rmc", weights.astype(jnp.bfloat16), keys_lat, preferred_element_type=jnp.float32
    )
    return (peak_val, weight_sum, summed)


def merge_pair(left_part, right_part):
    peak_left, total_left, sum_left = left_part
    peak_right, total_right, sum_right = right_part
    peak_val = jnp.maximum(peak_left, peak_right)
    factor_left = jnp.exp(peak_left - peak_val)
    factor_right = jnp.exp(peak_right - peak_val)
    weight_sum = factor_left * total_left + factor_right * total_right
    summed = factor_left[..., None] * sum_left + factor_right[..., None] * sum_right
    return (peak_val, weight_sum, summed)


def local(
    hidden_in,
    q_lat,
    q_rope,
    new_lat,
    new_rope,
    cache_lat,
    cache_rope,
    lengths,
    w_uv,
    w_out,
    norm_gain,
    w_router,
    routes,
    w_gate,
    w_up,
    w_down,
):
    requests, new_steps, head_count, latent_dim = q_lat.shape
    query_rows = new_steps * head_count
    query = q_lat.reshape(requests, query_rows, latent_dim)
    query_rope = q_rope.reshape(requests, query_rows, q_rope.shape[3])
    cache_span = cache_lat.shape[1]
    position = lax.axis_index("blk") * cache_span + lax.iota(jnp.int32, cache_span)
    cache_valid = jnp.broadcast_to(
        position[None, None, :] < lengths[:, None, None], (requests, query_rows, cache_span)
    )
    cache_part = block_partial(query, query_rope, cache_lat, cache_rope, cache_valid)
    token_of_row = lax.iota(jnp.int32, query_rows) // head_count
    fresh_valid = lax.iota(jnp.int32, new_steps)[None, :] <= token_of_row[:, None]
    fresh_valid = jnp.broadcast_to(fresh_valid[None, :, :], (requests, query_rows, new_steps))
    fresh_part = block_partial(query, query_rope, new_lat, new_rope, fresh_valid)
    merged = merged_2(cache_part, "blk", merge_pair)
    peak_val, weight_sum, summed = merge_pair(merged, fresh_part)
    lat_out = (summed / weight_sum[:, :, None]).astype(jnp.bfloat16)
    token_rows = requests * new_steps
    head_cols = w_uv.shape[1]
    head_pick = lax.axis_index("blk") * head_cols // V
    lat_heads = lat_out.reshape(requests, new_steps, head_count, latent_dim)
    lat_head = lax.dynamic_index_in_dim(lat_heads, head_pick, axis=2, keepdims=False).reshape(
        token_rows, latent_dim
    )
    heads_out = jnp.dot(lat_head, w_uv, preferred_element_type=jnp.float32).astype(jnp.bfloat16)
    proj_part = jnp.dot(heads_out, w_out, preferred_element_type=jnp.float32)
    projected = lax.psum(proj_part, "blk")
    width = hidden_in.shape[2]
    mixed = hidden_in.reshape(token_rows, width).astype(jnp.float32) + projected
    meansq = jnp.mean(mixed * mixed, axis=1, keepdims=True)
    normed = (mixed * lax.rsqrt(meansq + NORM_EPS) * norm_gain[None, :]).astype(jnp.bfloat16)
    affinity = jax.nn.sigmoid(jnp.dot(normed, w_router, preferred_element_type=jnp.float32))
    expert_total = w_router.shape[1]
    top_count = routes.shape[2]
    flat_routes = routes.reshape(token_rows, top_count)
    route_hits = flat_routes[:, :, None] == lax.iota(jnp.int32, expert_total)[None, None, :]
    chosen = jnp.sum(jnp.where(route_hits, affinity[:, None, :], 0.0), axis=2)
    route_weight = ROUTE_SCALE * chosen / jnp.sum(chosen, axis=1, keepdims=True)
    local_count = w_gate.shape[0]
    local_ids = lax.axis_index("blk") * local_count + lax.iota(jnp.int32, local_count)
    pair_routes = flat_routes.reshape(token_rows * top_count)
    local_hits = (pair_routes[:, None] == local_ids[None, :]).astype(jnp.int32)
    ranks = jnp.cumsum(local_hits, axis=0) - 1
    slot_ids = lax.iota(jnp.int32, CAP)
    slot_match = local_hits.T[:, None, :] * (ranks.T[:, None, :] == slot_ids[None, :, None]).astype(
        jnp.int32
    )
    select = slot_match.reshape(local_count, CAP, token_rows, top_count).astype(jnp.float32)
    dispatch_map = jnp.sum(select, axis=3)
    combine_map = jnp.sum(select * route_weight[None, None, :, :], axis=3)
    dispatched = jnp.einsum(
        "esr,rd->esd", dispatch_map.astype(jnp.bfloat16), normed, preferred_element_type=jnp.float32
    ).astype(jnp.bfloat16)
    piece = lax.all_gather(dispatched, "exp", axis=1, tiled=True)
    gate = jnp.einsum("erd,edf->erf", piece, w_gate, preferred_element_type=jnp.float32)
    upper = jnp.einsum("erd,edf->erf", piece, w_up, preferred_element_type=jnp.float32)
    hidden_all = (jax.nn.silu(gate) * upper).astype(jnp.bfloat16)
    partial_out = jnp.einsum("erf,efd->erd", hidden_all, w_down, preferred_element_type=jnp.float32)
    expert_out = lax.psum_scatter(partial_out, "exp", scatter_dimension=1, tiled=True)
    moe_part = jnp.einsum("esr,esd->rd", combine_map, expert_out, precision=lax.Precision.HIGHEST)
    moe_all = lax.psum(moe_part, "blk")
    result = (mixed + moe_all).astype(jnp.bfloat16)
    return result.reshape(requests, new_steps, width)


def solution(mesh):
    in_specs = (
        P("exp", None, None),
        P("exp", None, None, None),
        P("exp", None, None, None),
        P("exp", None, None),
        P("exp", None, None),
        P("exp", "blk", None),
        P("exp", "blk", None),
        P("exp"),
        P(None, "blk"),
        P("blk", None),
        P(),
        P(),
        P("exp", None, None),
        P("blk", None, "exp"),
        P("blk", None, "exp"),
        P("blk", "exp", None),
    )
    out_specs = P("exp", None, None)
    return jax.shard_map(local, mesh=mesh, in_specs=in_specs, out_specs=out_specs, check_vma=False)
```

profile of v0, /device:TPU:24, one launch (start us, length us, event | category | flops | bytes accessed | tf_op | source)
XLA Modules:
  0.0 1199.8 jit_solution(7835807839142678732)
XLA Ops:
  7.8 1.4 fusion.56
  11.8 70.6 %all-gather.5 = f32[64,4,64]{2,1,0:T(4,128)S(1)} all-gather(f32[1,4,64]{2,1,0:T(4,128)S(1)} %bitcast.74), channel_id=3, replica_groups=mesh['blk'=64,'exp'=8] {'blk'}, dimensions={0}, use_global_device_ids=true | all-gather | bytes 66560 | tf_op jit(solution)/shard_map/all_gather | solution.py:15
  82.4 61.4 %all-gather.4 = f32[64,4,64]{2,1,0:T(4,128)S(1)} all-gather(f32[1,4,64]{2,1,0:T(4,128)S(1)} %bitcast.73), channel_id=2, replica_groups=mesh['blk'=64,'exp'=8] {'blk'}, dimensions={0}, use_global_device_ids=true | all-gather | bytes 66560 | tf_op jit(solution)/shard_map/all_gather | solution.py:15
  146.7 65.1 %all-gather.9.cloned.1.call-done = f32[256,64,512]{2,1,0:T(8,128)} async-done(((f32[4,64,512]{2,1,0:T(8,128)}), f32[256,64,512]{2,1,0:T(8,128)}) %all-gather.9.cloned.1.call-update) | async-done | bytes 33554448 | tf_op jit(solution)/shard_map/all_gather | solution.py:15
  212.9 79.7 %while.19 = (s32[]{:T(128)}, f32[4,64]{1,0:T(4,128)S(1)}, f32[4,64]{1,0:T(4,128)S(1)}, f32[4,64,512]{2,1,0:T(8,128)S(1)}, f32[64,4,64]{2,1,0:T(4,128)S(1)}, /*in...) while((s32[]{:T(128)}, f32[4,64]{1,0:T(4,128)S(1)}, ...), condition=%wide.region_3.4_spmd, body=%wide.region_2.3_spmd.sunk | while | flops 394757 | bytes 1583255 | solution.py:21
  212.9 1.2 fusion.79
  214.2 1.2 fusion.79
  215.5 1.2 fusion.79
  216.7 1.2 fusion.79
  218.0 1.2 fusion.79
  219.3 1.2 fusion.79
  220.5 1.2 fusion.79
  221.8 1.2 fusion.79
  223.1 1.2 fusion.79
  224.3 1.2 fusion.79
  225.6 1.2 fusion.79
  226.9 1.2 fusion.79
  228.1 1.2 fusion.79
  229.4 1.2 fusion.79
  230.7 1.2 fusion.79
  231.9 1.2 fusion.79
  233.2 1.2 fusion.79
  234.4 1.2 fusion.79
  235.7 1.2 fusion.79
  237.0 1.2 fusion.79
  238.2 1.2 fusion.79
  239.5 1.2 fusion.79
  240.8 1.2 fusion.79
  242.0 1.2 fusion.79
  243.3 1.2 fusion.79
  244.6 1.2 fusion.79
  245.8 1.2 fusion.79
  247.1 1.2 fusion.79
  248.4 1.2 fusion.79
  249.6 1.2 fusion.79
  250.9 1.2 fusion.79
  252.2 1.2 fusion.79
  253.4 1.2 fusion.79
  254.7 1.2 fusion.79
  256.0 1.2 fusion.79
  259.8 1.2 fusion.79
  261.0 1.2 fusion.79
  262.3 1.2 fusion.79
  263.5 1.2 fusion.79
  268.6 1.2 fusion.79
  269.9 1.2 fusion.79
  271.1 1.2 fusion.79
  272.4 1.2 fusion.79
  276.2 1.2 fusion.79
  277.5 1.2 fusion.79
  278.7 1.2 fusion.79
  280.0 1.2 fusion.79
  283.8 1.2 fusion.79
  285.1 1.2 fusion.79
  286.3 1.2 fusion.79
  287.6 1.2 fusion.79
  293.8 1.9 fusion.15
  298.7 375.5 %all-reduce.5.cloned.1.call-done = f32[16,2048]{1,0:T(8,128)} async-done(((f32[16,2048]{1,0:T(8,128)}), f32[16,2048]{1,0:T(8,128)}) %all-reduce.5.cloned.1.call-update) | async-done | bytes 131088 | tf_op jit(solution)/shard_map/psum | solution.py:95
  677.6 34.2 %all-gather.6 = bf16[8,3,2048]{2,1,0:T(4,128)(2,1)S(1)} all-gather(bf16[1,3,2048]{2,1,0:T(4,128)(2,1)S(1)} %fusion.3), channel_id=5, replica_groups=mesh['blk'=64,'exp'=8] {'exp'}, dimensions={0}, use_global_device_ids=true | all-gather | bytes 110592 | tf_op jit(solution)/shard_map/all_gather | solution.py:122
  711.9 1.4 fusion.19
  713.3 2.0 convolution_bitcast_fusion
  716.3 1.3 dynamic-slice
  718.2 93.9 %all-reduce.9.cloned.1.call-done = f32[1,24,2048]{2,0,1:T(1,128)} async-done(((f32[1,24,2048]{2,0,1:T(1,128)}), f32[1,24,2048]{2,0,1:T(1,128)}) %all-reduce.9.cloned.1.call-update) | async-done | bytes 196624
  813.9 377.7 %all-reduce.7.cloned.1.call-done = f32[16,2048]{1,0:T(8,128)} async-done(((f32[16,2048]{1,0:T(8,128)}), f32[16,2048]{1,0:T(8,128)}) %all-reduce.7.cloned.1.call-update) | async-done | bytes 131088 | tf_op jit(solution)/shard_map/psum | solution.py:129
  (125 shorter events, 35.9 us)
Async XLA Ops:
  6.5 1.2 copy-start
  6.5 205.3 %all-gather.9.cloned.1.call-start = ((), (), s32[]{:S(2)}) async-start(), calls=%async_computation.2 | async-start | bytes 34078720 | tf_op jit(solution)/shard_map/all_gather | solution.py:15
  11.5 662.7 %all-reduce.5.cloned.1.call-start = ((), (), s32[]{:S(2)}) async-start(), calls=%async_computation | async-start | bytes 262144 | tf_op jit(solution)/shard_map/psum | solution.py:95
  295.7 516.5 %all-reduce.9.cloned.1.call-start = ((), (), s32[]{:S(2)}) async-start(), calls=%async_computation.3 | async-start | bytes 393216
  716.3 475.4 %all-reduce.7.cloned.1.call-start = ((), (), s32[]{:S(2)}) async-start(), calls=%async_computation.1 | async-start | bytes 262144 | tf_op jit(solution)/shard_map/psum | solution.py:129
Sparse Core Ops, SparseCore 0:
  11.6 200.1 all-gather.8
  295.8 378.3 all-reduce.4
  716.4 95.6 all-reduce.8
  814.9 376.7 all-reduce.6
where the time goes:
time: 1200 us
  waiting for transfers between devices  912 us (76%)
  blocking collectives  166 us (14%)
  other arithmetic  82.9 us (7%)
  matrix products  15.3 us (1%)
  between operations  13.9 us (1%)
    psum x1, waiting for transfers between devices, local(): moe_all = lax.psum(moe_part, 'blk')  378 us
    psum x1, waiting for transfers between devices, local(): projected = lax.psum(proj_part, 'blk')  376 us
    all_gather x2, blocking collectives, merged_2(): everything = jax.tree.map(lambda part: lax.all_gather(part, axis), x)  132 us
    unnamed x5, waiting for transfers between devices  94 us
    add x63, other arithmetic, merge_pair(): factor_left[..., None] * sum_left + factor_right[..., None] * sum_right  76.3 us
    all_gather x1, waiting for transfers between devices, merged_2(): everything = jax.tree.map(lambda part: lax.all_gather(part, axis), x)  65.1 us
    all_gather x1, blocking collectives, local(): piece = lax.all_gather(dispatched, 'exp', axis=1, tiled=True)  34.2 us
  transfers between devices with their start and end apart: 4, of which 4 were waited for; matrix products, arithmetic and copies ran while one was open for 1% of the time, Pallas kernels for 0%

commit v1 on v0

--- a/solution.py
+++ b/solution.py
@@ -119,7 +119,9 @@
     dispatched = jnp.einsum(
         "esr,rd->esd", dispatch_map.astype(jnp.bfloat16), normed, preferred_element_type=jnp.float32
     ).astype(jnp.bfloat16)
-    piece = lax.all_gather(dispatched, "exp", axis=1, tiled=True)
+    piece = jnp.concatenate(
+        lax.all_to_all(jnp.stack([dispatched] * lax.axis_size("exp")), "exp", 0, 0), axis=1
+    )
     gate = jnp.einsum("erd,edf->erf", piece, w_gate, preferred_element_type=jnp.float32)
     upper = jnp.einsum("erd,edf->erf", piece, w_up, preferred_element_type=jnp.float32)
     hidden_all = (jax.nn.silu(gate) * upper).astype(jnp.bfloat16)

time: 1200 us -> 1180 us (0.983)
  blocking collectives: 166 us -> 144 us
    all_gather x1 -> x0, blocking collectives: 34.2 us -> none  [local(): piece = lax.all_gather(dispatched, 'exp', axis=1, tiled=True)]
    all_to_all x0 -> x1, blocking collectives: none -> 12.1 us  [local(): lax.all_to_all(jnp.stack([dispatched] * lax.axis_size('exp')), 'exp', 0, 0)]
where the time goes in v1:
time: 1180 us
  waiting for transfers between devices  911 us (77%)
  blocking collectives  144 us (12%)
  other arithmetic  82.9 us (7%)
  matrix products  15.3 us (1%)
  between operations  13.9 us (1%)
    psum x1, waiting for transfers between devices, local(): moe_all = lax.psum(moe_part, 'blk')  378 us
    psum x1, waiting for transfers between devices, local(): projected = lax.psum(proj_part, 'blk')  376 us
    all_gather x2, blocking collectives, merged_2(): everything = jax.tree.map(lambda part: lax.all_gather(part, axis), x)  132 us
    unnamed x5, waiting for transfers between devices  92.8 us
    add x63, other arithmetic, merge_pair(): factor_left[..., None] * sum_left + factor_right[..., None] * sum_right  76.3 us
    all_gather x1, waiting for transfers between devices, merged_2(): everything = jax.tree.map(lambda part: lax.all_gather(part, axis), x)  65.1 us
  transfers between devices with their start and end apart: 4, of which 4 were waited for; matrix products, arithmetic and copies ran while one was open for 1% of the time, Pallas kernels for 0%

profile of v1, /device:TPU:24, one launch (start us, length us, event | category | flops | bytes accessed | tf_op | source)
XLA Modules:
  0.0 1176.6 jit_solution(10919101895567348391)
XLA Ops:
  7.8 1.4 fusion.55
  11.8 70.6 %all-gather.4 = f32[64,4,64]{2,1,0:T(4,128)S(1)} all-gather(f32[1,4,64]{2,1,0:T(4,128)S(1)} %bitcast.72), channel_id=3, replica_groups=mesh['blk'=64,'exp'=8] {'blk'}, dimensions={0}, use_global_device_ids=true | all-gather | bytes 66560 | tf_op jit(solution)/shard_map/all_gather | solution.py:15
  82.4 61.4 %all-gather.3 = f32[64,4,64]{2,1,0:T(4,128)S(1)} all-gather(f32[1,4,64]{2,1,0:T(4,128)S(1)} %bitcast.71), channel_id=2, replica_groups=mesh['blk'=64,'exp'=8] {'blk'}, dimensions={0}, use_global_device_ids=true | all-gather | bytes 66560 | tf_op jit(solution)/shard_map/all_gather | solution.py:15
  146.7 65.1 %all-gather.7.cloned.1.call-done = f32[256,64,512]{2,1,0:T(8,128)} async-done(((f32[4,64,512]{2,1,0:T(8,128)}), f32[256,64,512]{2,1,0:T(8,128)}) %all-gather.7.cloned.1.call-update) | async-done | bytes 33554448 | tf_op jit(solution)/shard_map/all_gather | solution.py:15
  212.9 79.7 %while.19 = (s32[]{:T(128)}, f32[4,64]{1,0:T(4,128)S(1)}, f32[4,64]{1,0:T(4,128)S(1)}, f32[4,64,512]{2,1,0:T(8,128)S(1)}, f32[64,4,64]{2,1,0:T(4,128)S(1)}, /*in...) while((s32[]{:T(128)}, f32[4,64]{1,0:T(4,128)S(1)}, ...), condition=%wide.region_3.4_spmd, body=%wide.region_2.3_spmd.sunk | while | flops 394757 | bytes 1583255 | solution.py:21
  212.9 1.2 fusion.78
  214.2 1.2 fusion.78
  215.5 1.2 fusion.78
  216.7 1.2 fusion.78
  218.0 1.2 fusion.78
  219.3 1.2 fusion.78
  220.5 1.2 fusion.78
  221.8 1.2 fusion.78
  223.1 1.2 fusion.78
  224.3 1.2 fusion.78
  225.6 1.2 fusion.78
  226.9 1.2 fusion.78
  228.1 1.2 fusion.78
  229.4 1.2 fusion.78
  230.7 1.2 fusion.78
  231.9 1.2 fusion.78
  233.2 1.2 fusion.78
  234.4 1.2 fusion.78
  235.7 1.2 fusion.78
  237.0 1.2 fusion.78
  238.2 1.2 fusion.78
  239.5 1.2 fusion.78
  240.8 1.2 fusion.78
  242.0 1.2 fusion.78
  243.3 1.2 fusion.78
  244.6 1.2 fusion.78
  245.8 1.2 fusion.78
  247.1 1.2 fusion.78
  248.4 1.2 fusion.78
  249.6 1.2 fusion.78
  250.9 1.2 fusion.78
  252.2 1.2 fusion.78
  253.4 1.2 fusion.78
  254.7 1.2 fusion.78
  256.0 1.2 fusion.78
  259.8 1.2 fusion.78
  261.0 1.2 fusion.78
  262.3 1.2 fusion.78
  263.5 1.2 fusion.78
  268.6 1.2 fusion.78
  269.9 1.2 fusion.78
  271.1 1.2 fusion.78
  272.4 1.2 fusion.78
  276.2 1.2 fusion.78
  277.5 1.2 fusion.78
  278.7 1.2 fusion.78
  280.0 1.2 fusion.78
  283.8 1.2 fusion.78
  285.1 1.2 fusion.78
  286.3 1.2 fusion.78
  287.6 1.2 fusion.78
  293.8 1.9 fusion.14
  298.7 375.5 %all-reduce.5.cloned.1.call-done = f32[16,2048]{1,0:T(8,128)} async-done(((f32[16,2048]{1,0:T(8,128)}), f32[16,2048]{1,0:T(8,128)}) %all-reduce.5.cloned.1.call-update) | async-done | bytes 131088 | tf_op jit(solution)/shard_map/psum | solution.py:95
  677.7 12.1 %all_to_all.5 = bf16[8,1,3,2048]{3,2,1,0:T(4,128)(2,1)S(1)} all-to-all(bf16[8,1,3,2048]{3,2,1,0:T(4,128)(2,1)S(1)} %stack.2), channel_id=1, replica_groups=mesh['blk'=64,'exp'=8] {'exp'}, dimensions={0} | all-to-all | bytes 196608 | tf_op jit(solution)/shard_map/all_to_all | solution.py:123
  689.9 1.4 fusion.18
  691.3 2.0 convolution_bitcast_fusion
  694.3 1.3 dynamic-slice
  696.2 92.7 %all-reduce.9.cloned.1.call-done = f32[1,24,2048]{2,0,1:T(1,128)} async-done(((f32[1,24,2048]{2,0,1:T(1,128)}), f32[1,24,2048]{2,0,1:T(1,128)}) %all-reduce.9.cloned.1.call-update) | async-done | bytes 196624
  790.7 377.7 %all-reduce.7.cloned.1.call-done = f32[16,2048]{1,0:T(8,128)} async-done(((f32[16,2048]{1,0:T(8,128)}), f32[16,2048]{1,0:T(8,128)}) %all-reduce.7.cloned.1.call-update) | async-done | bytes 131088 | tf_op jit(solution)/shard_map/psum | solution.py:131
  (126 shorter events, 36.0 us)
Async XLA Ops:
  6.5 1.2 copy-start
  6.5 205.3 %all-gather.7.cloned.1.call-start = ((), (), s32[]{:S(2)}) async-start(), calls=%async_computation.3 | async-start | bytes 34078720 | tf_op jit(solution)/shard_map/all_gather | solution.py:15
  11.5 662.7 %all-reduce.5.cloned.1.call-start = ((), (), s32[]{:S(2)}) async-start(), calls=%async_computation.1 | async-start | bytes 262144 | tf_op jit(solution)/shard_map/psum | solution.py:95
  295.7 493.3 %all-reduce.9.cloned.1.call-start = ((), (), s32[]{:S(2)}) async-start(), calls=%async_computation.4 | async-start | bytes 393216
  694.3 474.2 %all-reduce.7.cloned.1.call-start = ((), (), s32[]{:S(2)}) async-start(), calls=%async_computation.2 | async-start | bytes 262144 | tf_op jit(solution)/shard_map/psum | solution.py:131
Sparse Core Ops, SparseCore 0:
  11.6 200.1 all-gather.6
  295.8 378.3 all-reduce.4
  694.4 94.5 all-reduce.8
  791.7 376.7 all-reduce.6
